TPU v7x, 32 devices: a whole 2x2x4 slice. The times are simulated.
32 devices in a mesh: section: 8 (over z, core), seq: 4 (over y, x).
Axes of the slice: x: 2, y: 2, z: 4, core: 2. Of those that a mesh axis runs over, the one named last changes fastest.
Arguments:
- queries: bfloat16 [8, 512, 8192], P('section', 'seq'), may hold values from -48 to 48
- key_states: bfloat16 [8, 512, 1024], P('section', 'seq'), may hold values from -6 to 6
- section_value_states: bfloat16 [8, 512, 1024], P('section', 'seq'), may hold values from -6 to 6
- out_grad: bfloat16 [8, 512, 8192], P('section', 'seq'), may hold values from -1.5 to 1.5
- layer_input: bfloat16 [8, 512, 8192], P('section', 'seq'), may hold values from -6 to 6
- doc_segments: int32 [8, 512], P('section', 'seq'), may hold values from 0 to 3, never falling along the last dimension, each value on 1 to 256 neighbouring positions
Outputs:
- query_grad: bfloat16 [8, 512, 8192], P('section', 'seq')
- key_grad: bfloat16 [8, 512, 1024], P('section', 'seq')
- weight_grad: bfloat16 [8, 8192, 1024], P('section', None, 'seq')
Inputs may be any that keep to these rules, and one draw needn't show every extreme that they name: `doc_segments`: document numbers never fall along a section's positions; a document holds at most 256 positions.
All inputs are finite; a program needn't handle non-finite values.
Results may differ from a plain program's by a relative error of at most 0.012.
The roundings to bfloat16 on the way count: a program that leaves them out, or rounds other values in their place, can miss the bound.
Values may be sent and summed in bfloat16 or wider, within the bound.
No kernel may reach another device: no remote copies, remote signals or barrier semaphores. Data moves between devices by JAX's collectives and lax.ppermute only.
A program may use at most 128 MiB of HBM per device.

v0:
```python
import math
import jax
import jax.numpy as jnp
from jax import lax
from jax.sharding import PartitionSpec as P

HEAD_WIDTH = 128


def group_pass(query_group, key_col, value_col, grad_group, allowed):
    scale_factor = 1.0 / math.sqrt(key_col.shape[1])

    def one_head(totals, head_inputs):
        query_one, grad_one = head_inputs
        key_acc, value_acc = totals
        scores = jnp.dot(query_one, key_col.T, preferred_element_type=jnp.float32) * scale_factor
        scores = jnp.where(allowed, scores, -jnp.inf)
        row_max = jnp.max(scores, axis=1, keepdims=True)
        weights = jnp.exp(scores - row_max)
        attention = weights / jnp.sum(weights, axis=1, keepdims=True)
        probs_low = attention.astype(jnp.bfloat16)
        attended = jnp.dot(probs_low, value_col, preferred_element_type=jnp.float32).astype(
            jnp.bfloat16
        )
        attended = lax.optimization_barrier(attended)
        row_delta = jnp.sum(
            grad_one.astype(jnp.float32) * attended.astype(jnp.float32), axis=1, keepdims=True
        )
        dprobs = jnp.dot(grad_one, value_col.T, preferred_element_type=jnp.float32)
        dscores = (attention * (dprobs - row_delta) * scale_factor).astype(jnp.bfloat16)
        query_part = jnp.dot(dscores, key_col, preferred_element_type=jnp.float32).astype(
            jnp.bfloat16
        )
        key_acc = key_acc + jnp.dot(dscores.T, query_one, preferred_element_type=jnp.float32)
        value_acc = value_acc + jnp.dot(probs_low.T, grad_one, preferred_element_type=jnp.float32)
        return ((key_acc, value_acc), query_part)

    starting = jnp.zeros(key_col.shape, jnp.float32)
    (key_acc, value_acc), query_parts = lax.scan(
        one_head, (starting, starting), (query_group, grad_group)
    )
    return (query_parts, key_acc.astype(jnp.bfloat16), value_acc.astype(jnp.bfloat16))


def attention_grads(query_cols, key_cols, value_cols, grad_cols, doc_ids):
    length = query_cols.shape[0]
    kv_heads = key_cols.shape[1] // HEAD_WIDTH
    q_heads = query_cols.shape[1] // HEAD_WIDTH
    group_size = q_heads // kv_heads
    position = jnp.arange(length, dtype=jnp.int32)
    allowed = (position[:, None] >= position[None, :]) & (doc_ids[:, None] == doc_ids[None, :])
    query_split = query_cols.reshape(length, kv_heads, group_size, HEAD_WIDTH).transpose(1, 2, 0, 3)
    grad_split = grad_cols.reshape(length, kv_heads, group_size, HEAD_WIDTH).transpose(1, 2, 0, 3)
    key_split = key_cols.reshape(length, kv_heads, HEAD_WIDTH).transpose(1, 0, 2)
    value_split = value_cols.reshape(length, kv_heads, HEAD_WIDTH).transpose(1, 0, 2)

    def per_group(inputs):
        return group_pass(inputs[0], inputs[1], inputs[2], inputs[3], allowed)

    query_parts, key_parts, value_parts = lax.map(
        per_group, (query_split, key_split, value_split, grad_split)
    )
    query_out = query_parts.transpose(2, 0, 1, 3).reshape(length, q_heads * HEAD_WIDTH)
    key_out = key_parts.transpose(1, 0, 2).reshape(length, kv_heads * HEAD_WIDTH)
    value_out = value_parts.transpose(1, 0, 2).reshape(length, kv_heads * HEAD_WIDTH)
    return (query_out, key_out, value_out)


def row_product(shard_rows, value_rows):
    return lax.dot_general(
        shard_rows, value_rows, (((0,), (0,)), ((), ())), preferred_element_type=jnp.float32
    )


def local(queries, key_states, section_value_states, out_grad, layer_input, doc_segments):
    section_count = lax.axis_size("section")
    mirror = [(i, section_count - 1 - i) for i in range(section_count)]
    mirror_rows = lax.ppermute(layer_input[0], "section", mirror)
    query_head, key_head, value_head, grad_head = (
        lax.all_to_all(queries[0], "seq", split_axis=1, concat_axis=0, tiled=True),
        lax.all_to_all(key_states[0], "seq", split_axis=1, concat_axis=0, tiled=True),
        lax.all_to_all(section_value_states[0], "seq", split_axis=1, concat_axis=0, tiled=True),
        lax.all_to_all(out_grad[0], "seq", split_axis=1, concat_axis=0, tiled=True),
    )
    doc_ids = lax.all_gather(doc_segments[0], "seq", axis=0, tiled=True)
    query_out, key_out, value_out = attention_grads(
        query_head, key_head, value_head, grad_head, doc_ids
    )
    query_back, key_back = (
        lax.all_to_all(query_out, "seq", split_axis=0, concat_axis=1, tiled=True),
        lax.all_to_all(key_out, "seq", split_axis=0, concat_axis=1, tiled=True),
    )
    both_rows = jnp.concatenate([layer_input[0], mirror_rows], axis=0)
    gathered = lax.all_gather(both_rows, "seq", axis=0, tiled=True)
    mirror_value = lax.ppermute(value_out, "section", mirror)
    seq_count = lax.axis_size("seq")
    chunk = value_out.shape[0] // seq_count
    both_values = jnp.stack(
        [value_out.reshape(seq_count, chunk, -1), mirror_value.reshape(seq_count, chunk, -1)],
        axis=1,
    ).reshape(2 * value_out.shape[0], value_out.shape[1])
    paired = row_product(gathered, both_values)
    return (query_back[None], key_back[None], paired.astype(jnp.bfloat16)[None])


def solution(mesh):
    in_specs = (
        P("section", "seq", None),
        P("section", "seq", None),
        P("section", "seq", None),
        P("section", "seq", None),
        P("section", "seq", None),
        P("section", "seq"),
    )
    out_specs = (P("section", "seq", None), P("section", "seq", None), P("section", None, "seq"))
    return jax.shard_map(local, mesh=mesh, in_specs=in_specs, out_specs=out_specs, check_vma=False)
```

profile of v0, /device:TPU:8, one launch (start us, length us, event | category | flops | bytes accessed | tf_op | source)
XLA Modules:
  0.0 332.5 jit_solution(17759359656926367715)
XLA Ops:
  9.0 3.7 %all-to-all-start.2 = ((bf16[128,4,256]{2,0,1:T(8,128)(2,1)}), bf16[128,4,256]{2,0,1:T(8,128)(2,1)S(1)}, u32[]{:S(2)}, u32[]{:S(2)}) async-start(bf16[128,4,256]{2,0,1:T(8,128)(2,1)} %copy.27), calls=%async_computation.2 | async-start | bytes 524288 | tf_op jit(solution)/shard_map/all_to_all | solution.py:81
  14.6 3.5 %all-to-all-done.2 = bf16[128,4,256]{2,0,1:T(8,128)(2,1)S(1)} async-done(((bf16[128,4,256]{2,0,1:T(8,128)(2,1)}), bf16[128,4,256]{2,0,1:T(8,128)(2,1)S(1)}, u32[]{:S(2)}, u32[]{:S(2)}) %all-to-all-start.2) | async-done | bytes 262176 | tf_op jit(solution)/shard_map/all_to_all | solution.py:81
  18.1 3.4 %all-to-all-start.3 = ((bf16[128,4,256]{2,0,1:T(8,128)(2,1)}), bf16[128,4,256]{2,0,1:T(8,128)(2,1)S(1)}, u32[]{:S(2)}, u32[]{:S(2)}) async-start(bf16[128,4,256]{2,0,1:T(8,128)(2,1)} %copy.28), calls=%async_computation.3 | async-start | bytes 524288 | tf_op jit(solution)/shard_map/all_to_all | solution.py:82
  21.5 3.3 all_to_all.72
  27.3 4.2 %all-to-all-start = ((bf16[128,4,2048]{2,0,1:T(8,128)(2,1)}), bf16[128,4,2048]{2,0,1:T(8,128)(2,1)S(1)}, u32[]{:S(2)}, u32[]{:S(2)}) async-start(bf16[128,4,2048]{2,0,1:T(8,128)(2,1)} %copy.25), calls=%async_computation | async-start | bytes 4194304 | tf_op jit(solution)/shard_map/all_to_all | solution.py:80
  31.5 4.5 %all_to_all.75 = bf16[128,4,2048]{2,1,0:T(4,128)(2,1)} reshape(bf16[1,128,8192]{2,1,0:T(8,128)(2,1)} %param.13) | data formatting | bytes 4194304 | tf_op jit(solution)/shard_map/all_to_all | solution.py:83
  36.0 4.1 %copy.26 = bf16[128,4,2048]{2,0,1:T(8,128)(2,1)} copy(bf16[128,4,2048]{2,1,0:T(4,128)(2,1)} %all_to_all.75) | data formatting | bytes 4194304 | tf_op jit(solution)/shard_map/all_to_all | solution.py:83
  40.1 14.6 %all-to-all-done = bf16[128,4,2048]{2,0,1:T(8,128)(2,1)S(1)} async-done(((bf16[128,4,2048]{2,0,1:T(8,128)(2,1)}), bf16[128,4,2048]{2,0,1:T(8,128)(2,1)S(1)}, u32[]{:S(2)}, u32[]{:S(2)}) %all-to-all-start) | async-done | bytes 2097184 | tf_op jit(solution)/shard_map/all_to_all | solution.py:80
  54.7 4.4 %all-to-all-start.1 = ((bf16[128,4,2048]{2,0,1:T(8,128)(2,1)}), bf16[128,4,2048]{2,0,1:T(8,128)(2,1)}, u32[]{:S(2)}, u32[]{:S(2)}) async-start(bf16[128,4,2048]{2,0,1:T(8,128)(2,1)} %copy.26), calls=%async_computation.1 | async-start | bytes 4194304 | tf_op jit(solution)/shard_map/all_to_all | solution.py:83
  59.2 26.0 %all-gather = s32[1,512]{1,0:T(1,128)S(1)} all-gather(s32[1,128]{1,0:T(1,128)S(1)} %copy-done.8), channel_id=2, replica_groups=mesh['section'=8,'seq'=4] {'seq'}, dimensions={1}, use_global_device_ids=true | all-gather | bytes 2560 | tf_op jit(solution)/shard_map/all_gather | solution.py:85
  87.7 3.7 %copy.48 = bf16[64,8,16,128]{3,2,1,0:T(8,128)(2,1)} copy(bf16[64,8,16,128]{3,1,2,0:T(8,128)(2,1)} %bitcast.38) | data formatting | bytes 4194304
  91.4 33.2 %collective-permute-done = bf16[128,8192]{1,0:T(8,128)(2,1)} collective-permute-done((bf16[128,8192]{1,0:T(8,128)(2,1)}, bf16[128,8192]{1,0:T(8,128)(2,1)}, u32[]{:S(2)}, u32[]{:S(2)}) %collective-permute-start) | collective-permute-done | bytes 2097184 | tf_op jit(solution)/shard_map/ppermute | solution.py:78
  124.6 4.0 %pad_maximum_fusion = bf16[256,8192]{1,0:T(8,128)(2,1)} fusion(bf16[128,8192]{1,0:T(8,128)(2,1)} %collective-permute-done, bf16[128,8192]{1,0:T(8,128)(2,1)S(1)} %bitcast.127), kind=kLoop, calls=%fused_computation.43 | loop fusion | flops 8388608 | bytes 8388608 | tf_op jit(solution)/shard_map/concatenate | solution.py:93
  128.6 110.8 %while.32 = (s32[]{:T(128)}, bf16[2,8,512,128]{3,2,1,0:T(8,128)(2,1)}, bf16[2,512,128]{2,1,0:T(8,128)(2,1)}, bf16[2,512,128]{2,1,0:T(8,128)(2,1)}, bf16[2,8,512,...) while((s32[]{:T(128)}, ...), condition=%wide.region_6.7_spmd.clone, body=%wide.region_0.6_spmd.clone.sunk | while | flops 407894528 | bytes 49566240 | solution.py:60
  132.8 48.1 %while.33 = (s32[]{:T(128)}, f32[512,128]{1,0:T(8,128)S(1)}, f32[512,128]{1,0:T(8,128)S(1)}, bf16[8,512,128]{2,1,0:T(8,128)(2,1)}, bf16[8,512,128]{2,1,0:T(8,128...) while((s32[]{:T(128)}, f32[512,128]{1,0:T(8,128)S(1)}, ...), condition=%wide.region_5.5_spmd.clone, body=%wide.region_1.4_spmd.clone.sunk | while | flops 406977024 | bytes 10242200 | solution.py:39
  188.2 48.1 %while.33 = (s32[]{:T(128)}, f32[512,128]{1,0:T(8,128)S(1)}, f32[512,128]{1,0:T(8,128)S(1)}, bf16[8,512,128]{2,1,0:T(8,128)(2,1)}, bf16[8,512,128]{2,1,0:T(8,128...) while((s32[]{:T(128)}, f32[512,128]{1,0:T(8,128)S(1)}, ...), condition=%wide.region_5.5_spmd.clone, body=%wide.region_1.4_spmd.clone.sunk | while | flops 406977024 | bytes 10242200 | solution.py:39
  241.5 4.2 %all-to-all-start.5 = ((bf16[4,128,256]{2,1,0:T(8,128)(2,1)}), bf16[4,128,256]{2,1,0:T(8,128)(2,1)S(1)}, u32[]{:S(2)}, u32[]{:S(2)}) async-start(bf16[4,128,256]{2,1,0:T(8,128)(2,1)} %all_to_all.87), calls=%async_computation.5 | async-start | bytes 524288 | tf_op jit(solution)/shard_map/all_to_all | solution.py:91
  245.8 2.9 copy.33
  251.0 3.8 %all-to-all-done.5 = bf16[4,128,256]{2,1,0:T(8,128)(2,1)S(1)} async-done(((bf16[4,128,256]{2,1,0:T(8,128)(2,1)}), bf16[4,128,256]{2,1,0:T(8,128)(2,1)S(1)}, u32[]{:S(2)}, u32[]{:S(2)}) %all-to-all-start.5) | async-done | bytes 262176 | tf_op jit(solution)/shard_map/all_to_all | solution.py:91
  254.8 3.8 %all-to-all-start.4 = ((bf16[4,128,2048]{2,1,0:T(8,128)(2,1)}), bf16[4,128,2048]{2,1,0:T(8,128)(2,1)S(1)}, u32[]{:S(2)}, u32[]{:S(2)}) async-start(bf16[4,128,2048]{2,1,0:T(8,128)(2,1)} %all_to_all.84), calls=%async_computation.4 | async-start | bytes 4194304 | tf_op jit(solution)/shard_map/all_to_all | solution.py:90
  260.9 6.7 %collective-permute-done.1 = bf16[512,256]{0,1:T(8,128)(2,1)S(1)} collective-permute-done((bf16[512,256]{0,1:T(8,128)(2,1)}, bf16[512,256]{0,1:T(8,128)(2,1)S(1)}, u32[]{:S(2)}, u32[]{:S(2)}) %collective-permute-start.1) | collective-permute-done | bytes 262176 | tf_op jit(solution)/shard_map/ppermute | solution.py:95
  267.9 38.7 %all-to-all-done.4 = bf16[4,128,2048]{2,1,0:T(8,128)(2,1)S(1)} async-done(((bf16[4,128,2048]{2,1,0:T(8,128)(2,1)}), bf16[4,128,2048]{2,1,0:T(8,128)(2,1)S(1)}, u32[]{:S(2)}, u32[]{:S(2)}) %all-to-all-start.4) | async-done | bytes 2097184 | tf_op jit(solution)/shard_map/all_to_all | solution.py:90
  309.0 4.1 %copy.41 = bf16[1,128,8192]{2,1,0:T(8,128)(2,1)} copy(bf16[1,128,8192]{1,2,0:T(8,128)(2,1)} %bitcast.124) | data formatting | bytes 4194304
  313.1 12.6 %fusion.24 = bf16[1,8192,256]{2,1,0:T(8,128)(2,1)} fusion(bf16[1024,8192]{1,0:T(8,128)(2,1)} %all-gather.3.cloned.1.call-done, bf16[1024,256]{1,0:T(8,128)(2,1)S(1)} %bitcast.136), kind=kOutput, calls=%fused_computation.42 | convolution fusion | flops 4297064448 | bytes 21495808 | tf_op jit(solution)/shard_map/dot_general | solution.py:70
  (228 shorter events, 128.0 us)
Async XLA Ops:
  9.0 9.1 %all-to-all-start.2 = ((bf16[128,4,256]{2,0,1:T(8,128)(2,1)}), bf16[128,4,256]{2,0,1:T(8,128)(2,1)S(1)}, u32[]{:S(2)}, u32[]{:S(2)}) async-start(bf16[128,4,256]{2,0,1:T(8,128)(2,1)} %copy.27), calls=%async_computation.2 | async-start | bytes 524288 | tf_op jit(solution)/shard_map/all_to_all | solution.py:81
  18.1 9.2 %all-to-all-start.3 = ((bf16[128,4,256]{2,0,1:T(8,128)(2,1)}), bf16[128,4,256]{2,0,1:T(8,128)(2,1)S(1)}, u32[]{:S(2)}, u32[]{:S(2)}) async-start(bf16[128,4,256]{2,0,1:T(8,128)(2,1)} %copy.28), calls=%async_computation.3 | async-start | bytes 524288 | tf_op jit(solution)/shard_map/all_to_all | solution.py:82
  27.3 27.3 %all-to-all-start = ((bf16[128,4,2048]{2,0,1:T(8,128)(2,1)}), bf16[128,4,2048]{2,0,1:T(8,128)(2,1)S(1)}, u32[]{:S(2)}, u32[]{:S(2)}) async-start(bf16[128,4,2048]{2,0,1:T(8,128)(2,1)} %copy.25), calls=%async_computation | async-start | bytes 4194304 | tf_op jit(solution)/shard_map/all_to_all | solution.py:80
  31.5 93.1 %collective-permute-start = (bf16[128,8192]{1,0:T(8,128)(2,1)}, bf16[128,8192]{1,0:T(8,128)(2,1)}, u32[]{:S(2)}, u32[]{:S(2)}) collective-permute-start(bf16[128,8192]{1,0:T(8,128)(2,1)} %bitcast.126), channel_id=1, source_target_pairs={{0,28},{4,24},{8,20},{12,16},{16,12},{20,8},{24,4},{28,0},{1,29},{... | collective-permute-start | bytes 6291464 | tf_op jit(solution)/shard_map/ppermute | solution.py:78
  40.1 19.1 %copy-start.8 = (s32[1,128]{1,0:T(1,128)S(1)}, s32[1,128]{1,0:T(1,128)}, u32[]{:S(2)}) copy-start(s32[1,128]{1,0:T(1,128)} %param.15) | copy-start | bytes 1540
  54.7 4.5 %copy-start.3 = (bf16[128,4,2048]{2,0,1:T(8,128)(2,1)}, bf16[128,4,2048]{2,0,1:T(8,128)(2,1)S(1)}, u32[]{:S(2)}) copy-start(bf16[128,4,2048]{2,0,1:T(8,128)(2,1)S(1)} %all-to-all-done) | copy-start | bytes 6291460
  54.7 33.0 %all-to-all-start.1 = ((bf16[128,4,2048]{2,0,1:T(8,128)(2,1)}), bf16[128,4,2048]{2,0,1:T(8,128)(2,1)}, u32[]{:S(2)}, u32[]{:S(2)}) async-start(bf16[128,4,2048]{2,0,1:T(8,128)(2,1)} %copy.26), calls=%async_computation.1 | async-start | bytes 4194304 | tf_op jit(solution)/shard_map/all_to_all | solution.py:83
  59.1 253.9 %all-gather.3.cloned.1.call-start = ((), (), s32[]{:S(2)}) async-start(), calls=%async_computation.6 | async-start | bytes 20971520 | tf_op jit(solution)/shard_map/all_gather | solution.py:94
  87.7 36.9 %copy-start.6 = (bf16[1,128,8192]{2,1,0:T(8,128)(2,1)S(1)}, bf16[1,128,8192]{2,1,0:T(8,128)(2,1)}, u32[]{:S(2)}) copy-start(bf16[1,128,8192]{2,1,0:T(8,128)(2,1)} %param.14) | copy-start | bytes 6291460
  128.6 1.3 copy-start
  128.7 4.1 %copy-start.4 = (bf16[2,512,128]{2,1,0:T(8,128)(2,1)}, bf16[2,512,128]{2,1,0:T(8,128)(2,1)S(1)}, u32[]{:S(2)}) copy-start(bf16[2,512,128]{2,1,0:T(8,128)(2,1)S(1)} %get-tuple-element.437) | copy-start | bytes 786436 | tf_op jit(solution)/shard_map/while
  129.9 1.6 copy-start.2
  180.9 3.2 copy-start.1
  180.9 3.2 copy-start.5
  184.1 1.3 copy-start
  184.1 4.1 %copy-start.4 = (bf16[2,512,128]{2,1,0:T(8,128)(2,1)}, bf16[2,512,128]{2,1,0:T(8,128)(2,1)S(1)}, u32[]{:S(2)}) copy-start(bf16[2,512,128]{2,1,0:T(8,128)(2,1)S(1)} %get-tuple-element.437) | copy-start | bytes 786436 | tf_op jit(solution)/shard_map/while
  185.4 1.6 copy-start.2
  236.3 3.2 copy-start.1
  236.3 3.2 copy-start.5
  241.5 13.3 %all-to-all-start.5 = ((bf16[4,128,256]{2,1,0:T(8,128)(2,1)}), bf16[4,128,256]{2,1,0:T(8,128)(2,1)S(1)}, u32[]{:S(2)}, u32[]{:S(2)}) async-start(bf16[4,128,256]{2,1,0:T(8,128)(2,1)} %all_to_all.87), calls=%async_computation.5 | async-start | bytes 524288 | tf_op jit(solution)/shard_map/all_to_all | solution.py:91
  251.0 7.6 %copy-start.7 = (bf16[2,512,128]{2,1,0:T(8,128)(2,1)S(1)}, bf16[2,512,128]{2,1,0:T(8,128)(2,1)}, u32[]{:S(2)}) copy-start(bf16[2,512,128]{2,1,0:T(8,128)(2,1)} %get-tuple-element.103) | copy-start | bytes 786436
  254.8 51.7 %all-to-all-start.4 = ((bf16[4,128,2048]{2,1,0:T(8,128)(2,1)}), bf16[4,128,2048]{2,1,0:T(8,128)(2,1)S(1)}, u32[]{:S(2)}, u32[]{:S(2)}) async-start(bf16[4,128,2048]{2,1,0:T(8,128)(2,1)} %all_to_all.84), calls=%async_computation.4 | async-start | bytes 4194304 | tf_op jit(solution)/shard_map/all_to_all | solution.py:90
  259.4 8.2 %collective-permute-start.1 = (bf16[512,256]{0,1:T(8,128)(2,1)}, bf16[512,256]{0,1:T(8,128)(2,1)S(1)}, u32[]{:S(2)}, u32[]{:S(2)}) collective-permute-start(bf16[512,256]{0,1:T(8,128)(2,1)} %bitcast.18), channel_id=1, source_target_pairs={{0,28},{4,24},{8,20},{12,16},{16,12},{20,8},{24,4},{28,0},{1,29},{... | collective-permute-start | bytes 786440 | tf_op jit(solution)/shard_map/ppermute | solution.py:95
Sparse Core Ops, SparseCore 0:
  128.7 182.3 all-gather.2
where the time goes:
time: 335 us; the launch traced here: 333 us
  waiting for transfers between devices  100 us (30%)
  matrix products  85 us (25%)
  local copies, waits for them, and re-layouts  53.2 us (16%)
  other arithmetic  29 us (9%)
  blocking collectives  26 us (8%)
  starting transfers between devices  23.8 us (7%)
  between operations  14.2 us (4%)
    all_to_all x1, waiting for transfers between devices, local(): lax.all_to_all(query_out, 'seq', split_axis=0, concat_axis=1, tiled=True)  38.7 us
    ppermute x1, waiting for transfers between devices, local(): mirror_rows = lax.ppermute(layer_input[0], 'section', mirror)  33.2 us
    all_gather x1, blocking collectives, local(): doc_ids = lax.all_gather(doc_segments[0], 'seq', axis=0, tiled=True)  26 us
    dot_general x16, matrix products, one_head(): dprobs = jnp.dot(grad_one, value_col.T, preferred_element_type=jnp.float32)  20.4 us
    dot_general x16, matrix products, one_head(): jnp.dot(probs_low.T, grad_one, preferred_element_type=jnp.float32)  19.7 us
    reduce_sum x16, other arithmetic, one_head(): jnp.sum(grad_one.astype(jnp.float32) * attended.astype(jnp.float32), axis...  17.2 us
    dot_general x16, matrix products, one_head(): jnp.dot(dscores, key_col, preferred_element_type=jnp.float32)  16.1 us
    all_to_all x1, waiting for transfers between devices, local(): lax.all_to_all(queries[0], 'seq', split_axis=1, concat_axis=0, tiled=True)  14.6 us
  transfers between devices with their start and end apart: 9, of which 6 were waited for; matrix products, arithmetic and copies ran while one was open for 40% of the time, Pallas kernels for 0%

commit v1 on v0

--- a/solution.py
+++ b/solution.py
@@ -5,6 +5,22 @@
 from jax.sharding import PartitionSpec as P
 
 HEAD_WIDTH = 128
+
+
+def swapped_with_each(x, axis, split, join):
+    ways, here = (lax.axis_size(axis), lax.axis_index(axis))
+    width = x.shape[split] // ways
+    dims = list(x.shape)
+    dims[split] = width
+    height = dims[join]
+    dims[join] = height * ways
+    full = jnp.zeros(dims, x.dtype)
+    for mask in range(ways):
+        part = lax.dynamic_slice_in_dim(x, (here ^ mask) * width, width, axis=split)
+        if mask:
+            part = lax.ppermute(part, axis, [(d, d ^ mask) for d in range(ways)])
+        full = lax.dynamic_update_slice_in_dim(full, part, (here ^ mask) * height, axis=join)
+    return full
 
 
 def group_pass(query_group, key_col, value_col, grad_group, allowed):
@@ -77,7 +93,7 @@
     mirror = [(i, section_count - 1 - i) for i in range(section_count)]
     mirror_rows = lax.ppermute(layer_input[0], "section", mirror)
     query_head, key_head, value_head, grad_head = (
-        lax.all_to_all(queries[0], "seq", split_axis=1, concat_axis=0, tiled=True),
+        swapped_with_each(queries[0], "seq", 1, 0),
         lax.all_to_all(key_states[0], "seq", split_axis=1, concat_axis=0, tiled=True),
         lax.all_to_all(section_value_states[0], "seq", split_axis=1, concat_axis=0, tiled=True),
         lax.all_to_all(out_grad[0], "seq", split_axis=1, concat_axis=0, tiled=True),

time: 335 us -> 312 us (0.931)
  waiting for transfers between devices: 100 us -> 64.3 us
  blocking collectives: 26 us -> 33.7 us
  local copies, waits for them, and re-layouts: 53.2 us -> 59.6 us
    ppermute x1, waiting for transfers between devices: 33.2 us -> 11.5 us  [local(): mirror_rows = lax.ppermute(layer_input[0], 'section', mirror)]
    all_to_all x1 -> x0, waiting for transfers between devices: 14.6 us -> none  [local(): lax.all_to_all(queries[0], 'seq', split_axis=1, concat_axis=0, tiled=True)]
    dynamic_slice x0 -> x5, local copies, waits for them, and re-layouts: none -> 8.02 us  [swapped_with_each(): part = lax.dynamic_slice_in_dim(x, (here ^ mask) * width, width, axis=split)]
    all_gather x1, blocking collectives: 26 us -> 33.7 us  [local(): doc_ids = lax.all_gather(doc_segments[0], 'seq', axis=0, tiled=True)]
    dynamic_update_slice x0 -> x4, local copies, waits for them, and re-layouts: none -> 6.68 us  [swapped_with_each(): lax.dynamic_update_slice_in_dim(full, part, (here ^ mask) * height, axis=...]
    dynamic_slice x8, local copies, waits for them, and re-layouts: 2.85 us -> 9.09 us  [attention_grads(): lax.map(per_group, (query_split, key_split, value_split, grad_split))]
    all_to_all x2 -> x0, local copies, waits for them, and re-layouts: 5.79 us -> none  [local(): lax.all_to_all(queries[0], 'seq', split_axis=1, concat_axis=0, tiled=True)]
    all_to_all x1 -> x0, starting transfers between devices: 4.15 us -> none  [local(): lax.all_to_all(queries[0], 'seq', split_axis=1, concat_axis=0, tiled=True)]
  transfers between devices with their start and end apart: 9 -> 11, of which waited for: 6 -> 5; matrix products, arithmetic and copies ran while one was open for 40% -> 47% of each run, Pallas kernels for 0% -> 0%
where the time goes in v1:
time: 312 us; the launch traced here: 309 us
  matrix products  85 us (27%)
  waiting for transfers between devices  64.3 us (21%)
  local copies, waits for them, and re-layouts  59.6 us (19%)
  blocking collectives  33.7 us (11%)
  other arithmetic  27.7 us (9%)
  starting transfers between devices  23.9 us (8%)
  between operations  14.2 us (5%)
    all_to_all x1, waiting for transfers between devices, local(): lax.all_to_all(query_out, 'seq', split_axis=0, concat_axis=1, tiled=True)  38.3 us
    all_gather x1, blocking collectives, local(): doc_ids = lax.all_gather(doc_segments[0], 'seq', axis=0, tiled=True)  33.7 us
    dot_general x16, matrix products, one_head(): dprobs = jnp.dot(grad_one, value_col.T, preferred_element_type=jnp.float32)  20.4 us
    dot_general x16, matrix products, one_head(): jnp.dot(probs_low.T, grad_one, preferred_element_type=jnp.float32)  19.7 us
    reduce_sum x16, other arithmetic, one_head(): jnp.sum(grad_one.astype(jnp.float32) * attended.astype(jnp.float32), axis...  17.2 us
    dot_general x16, matrix products, one_head(): jnp.dot(dscores, key_col, preferred_element_type=jnp.float32)  16.1 us
    dot_general x1, matrix products, row_product(): lax.dot_general(shard_rows, value_rows, (((0,), (0,)), ((), ())), preferr...  12.6 us
    ppermute x1, waiting for transfers between devices, local(): mirror_rows = lax.ppermute(layer_input[0], 'section', mirror)  11.5 us
  transfers between devices with their start and end apart: 11, of which 5 were waited for; matrix products, arithmetic and copies ran while one was open for 47% of the time, Pallas kernels for 0%

profile of v1, /device:TPU:8, one launch (start us, length us, event | category | flops | bytes accessed | tf_op | source)
XLA Modules:
  0.0 309.3 jit_solution(12901176355108206026)
XLA Ops:
  10.1 3.7 %all-to-all-start.1 = ((bf16[128,4,256]{2,0,1:T(8,128)(2,1)}), bf16[128,4,256]{2,0,1:T(8,128)(2,1)S(1)}, u32[]{:S(2)}, u32[]{:S(2)}) async-start(bf16[128,4,256]{2,0,1:T(8,128)(2,1)} %copy.33), calls=%async_computation.1 | async-start | bytes 524288 | tf_op jit(solution)/shard_map/all_to_all | solution.py:97
  15.7 4.2 %all-to-all-done.1 = bf16[128,4,256]{2,0,1:T(8,128)(2,1)S(1)} async-done(((bf16[128,4,256]{2,0,1:T(8,128)(2,1)}), bf16[128,4,256]{2,0,1:T(8,128)(2,1)S(1)}, u32[]{:S(2)}, u32[]{:S(2)}) %all-to-all-start.1) | async-done | bytes 262176 | tf_op jit(solution)/shard_map/all_to_all | solution.py:97
  19.9 3.4 %all-to-all-start.2 = ((bf16[128,4,256]{2,0,1:T(8,128)(2,1)}), bf16[128,4,256]{2,0,1:T(8,128)(2,1)S(1)}, u32[]{:S(2)}, u32[]{:S(2)}) async-start(bf16[128,4,256]{2,0,1:T(8,128)(2,1)} %copy.34), calls=%async_computation.2 | async-start | bytes 524288 | tf_op jit(solution)/shard_map/all_to_all | solution.py:98
  23.3 3.3 %all_to_all.60 = bf16[128,4,2048]{2,1,0:T(4,128)(2,1)S(1)} reshape(bf16[1,128,8192]{2,1,0:T(8,128)(2,1)} %param.13) | data formatting | bytes 4194304 | tf_op jit(solution)/shard_map/all_to_all | solution.py:99
  26.6 2.5 copy.32
  29.1 4.2 %all-to-all-start = ((bf16[128,4,2048]{2,0,1:T(8,128)(2,1)}), bf16[128,4,2048]{2,0,1:T(8,128)(2,1)S(1)}, u32[]{:S(2)}, u32[]{:S(2)}) async-start(bf16[128,4,2048]{2,0,1:T(8,128)(2,1)} %copy.32), calls=%async_computation | async-start | bytes 4194304 | tf_op jit(solution)/shard_map/all_to_all | solution.py:99
  33.3 2.7 constant_dynamic-slice_fusion.2
  47.1 33.7 %all-gather = s32[1,512]{1,0:T(1,128)S(1)} all-gather(s32[1,128]{1,0:T(1,128)S(1)} %copy-done.10), channel_id=2, replica_groups=mesh['section'=8,'seq'=4] {'seq'}, dimensions={1}, use_global_device_ids=true | all-gather | bytes 2560 | tf_op jit(solution)/shard_map/all_gather | solution.py:101
  88.8 11.5 %collective-permute-done.3 = bf16[128,8192]{1,0:T(8,128)(2,1)} collective-permute-done((bf16[128,8192]{1,0:T(8,128)(2,1)}, bf16[128,8192]{1,0:T(8,128)(2,1)}, u32[]{:S(2)}, u32[]{:S(2)}) %collective-permute-start.3) | collective-permute-done | bytes 2097184 | tf_op jit(solution)/shard_map/ppermute | solution.py:94
  100.3 4.0 %pad_maximum_fusion = bf16[256,8192]{1,0:T(8,128)(2,1)} fusion(bf16[128,8192]{1,0:T(8,128)(2,1)} %collective-permute-done.3, bf16[128,8192]{1,0:T(8,128)(2,1)S(1)} %bitcast.125), kind=kLoop, calls=%fused_computation.42 | loop fusion | flops 8388608 | bytes 8388608 | tf_op jit(solution)/shard_map/concatenate | solution.py:109
  104.3 112.3 %while.32 = (s32[]{:T(128)}, bf16[2,8,512,128]{3,2,1,0:T(8,128)(2,1)}, bf16[2,512,128]{2,1,0:T(8,128)(2,1)}, bf16[2,512,128]{2,1,0:T(8,128)(2,1)}, bf16[2,8,512,...) while((s32[]{:T(128)}, ...), condition=%wide.region_6.7_spmd.clone, body=%wide.region_0.6_spmd.clone.sunk | while | flops 407894528 | bytes 28594748 | solution.py:76
  109.2 48.1 %while.33 = (s32[]{:T(128)}, f32[512,128]{1,0:T(8,128)S(1)}, f32[512,128]{1,0:T(8,128)S(1)}, bf16[8,512,128]{2,1,0:T(8,128)(2,1)}, bf16[8,512,128]{2,1,0:T(8,128...) while((s32[]{:T(128)}, f32[512,128]{1,0:T(8,128)S(1)}, ...), condition=%wide.region_5.5_spmd.clone, body=%wide.region_1.4_spmd.clone.sunk | while | flops 406977024 | bytes 10242200 | solution.py:55
  157.4 2.3 bitcast_dynamic-update-slice_fusion.6
  165.4 48.0 %while.33 = (s32[]{:T(128)}, f32[512,128]{1,0:T(8,128)S(1)}, f32[512,128]{1,0:T(8,128)S(1)}, bf16[8,512,128]{2,1,0:T(8,128)(2,1)}, bf16[8,512,128]{2,1,0:T(8,128...) while((s32[]{:T(128)}, f32[512,128]{1,0:T(8,128)S(1)}, ...), condition=%wide.region_5.5_spmd.clone, body=%wide.region_1.4_spmd.clone.sunk | while | flops 406977024 | bytes 10242200 | solution.py:55
  213.5 2.3 bitcast_dynamic-update-slice_fusion.6
  218.8 3.7 %all-to-all-start.4 = ((bf16[4,128,256]{2,1,0:T(8,128)(2,1)}), bf16[4,128,256]{2,1,0:T(8,128)(2,1)S(1)}, u32[]{:S(2)}, u32[]{:S(2)}) async-start(bf16[4,128,256]{2,1,0:T(8,128)(2,1)} %all_to_all.72), calls=%async_computation.4 | async-start | bytes 524288 | tf_op jit(solution)/shard_map/all_to_all | solution.py:107
  222.5 2.9 copy.39
  227.7 3.8 %all-to-all-done.4 = bf16[4,128,256]{2,1,0:T(8,128)(2,1)S(1)} async-done(((bf16[4,128,256]{2,1,0:T(8,128)(2,1)}), bf16[4,128,256]{2,1,0:T(8,128)(2,1)S(1)}, u32[]{:S(2)}, u32[]{:S(2)}) %all-to-all-start.4) | async-done | bytes 262176 | tf_op jit(solution)/shard_map/all_to_all | solution.py:107
  231.6 3.8 %all-to-all-start.3 = ((bf16[4,128,2048]{2,1,0:T(8,128)(2,1)}), bf16[4,128,2048]{2,1,0:T(8,128)(2,1)S(1)}, u32[]{:S(2)}, u32[]{:S(2)}) async-start(bf16[4,128,2048]{2,1,0:T(8,128)(2,1)} %all_to_all.69), calls=%async_computation.3 | async-start | bytes 4194304 | tf_op jit(solution)/shard_map/all_to_all | solution.py:106
  238.3 6.5 %collective-permute-done.4 = bf16[512,256]{0,1:T(8,128)(2,1)S(1)} collective-permute-done((bf16[512,256]{0,1:T(8,128)(2,1)}, bf16[512,256]{0,1:T(8,128)(2,1)S(1)}, u32[]{:S(2)}, u32[]{:S(2)}) %collective-permute-start.4) | collective-permute-done | bytes 262176 | tf_op jit(solution)/shard_map/ppermute | solution.py:111
  245.0 38.3 %all-to-all-done.3 = bf16[4,128,2048]{2,1,0:T(8,128)(2,1)S(1)} async-done(((bf16[4,128,2048]{2,1,0:T(8,128)(2,1)}), bf16[4,128,2048]{2,1,0:T(8,128)(2,1)S(1)}, u32[]{:S(2)}, u32[]{:S(2)}) %all-to-all-start.3) | async-done | bytes 2097184 | tf_op jit(solution)/shard_map/all_to_all | solution.py:106
  283.3 2.5 copy.40
  285.8 4.1 %copy.47 = bf16[1,128,8192]{2,1,0:T(8,128)(2,1)} copy(bf16[1,128,8192]{1,2,0:T(8,128)(2,1)} %bitcast.122) | data formatting | bytes 4194304
  289.9 12.6 %fusion.24 = bf16[1,8192,256]{2,1,0:T(8,128)(2,1)} fusion(bf16[1024,8192]{1,0:T(8,128)(2,1)} %all-gather.3.cloned.1.call-done, bf16[1024,256]{1,0:T(8,128)(2,1)S(1)} %bitcast.137), kind=kOutput, calls=%fused_computation.41 | convolution fusion | flops 4297064448 | bytes 21495808 | tf_op jit(solution)/shard_map/dot_general | solution.py:86
  (245 shorter events, 138.2 us)
Async XLA Ops:
  7.2 93.1 %collective-permute-start.3 = (bf16[128,8192]{1,0:T(8,128)(2,1)}, bf16[128,8192]{1,0:T(8,128)(2,1)}, u32[]{:S(2)}, u32[]{:S(2)}) collective-permute-start(bf16[128,8192]{1,0:T(8,128)(2,1)} %bitcast.124), channel_id=1, source_target_pairs={{0,28},{4,24},{8,20},{12,16},{16,12},{20,8},{24,4},{28,0},{1,29},{... | collective-permute-start | bytes 6291464 | tf_op jit(solution)/shard_map/ppermute | solution.py:94
  10.1 9.8 %all-to-all-start.1 = ((bf16[128,4,256]{2,0,1:T(8,128)(2,1)}), bf16[128,4,256]{2,0,1:T(8,128)(2,1)S(1)}, u32[]{:S(2)}, u32[]{:S(2)}) async-start(bf16[128,4,256]{2,0,1:T(8,128)(2,1)} %copy.33), calls=%async_computation.1 | async-start | bytes 524288 | tf_op jit(solution)/shard_map/all_to_all | solution.py:97
  19.9 9.2 %all-to-all-start.2 = ((bf16[128,4,256]{2,0,1:T(8,128)(2,1)}), bf16[128,4,256]{2,0,1:T(8,128)(2,1)S(1)}, u32[]{:S(2)}, u32[]{:S(2)}) async-start(bf16[128,4,256]{2,0,1:T(8,128)(2,1)} %copy.34), calls=%async_computation.2 | async-start | bytes 524288 | tf_op jit(solution)/shard_map/all_to_all | solution.py:98
  29.1 4.2 %copy-start.3 = (bf16[128,4,256]{2,0,1:T(8,128)(2,1)}, bf16[128,4,256]{2,0,1:T(8,128)(2,1)S(1)}, u32[]{:S(2)}) copy-start(bf16[128,4,256]{2,0,1:T(8,128)(2,1)S(1)} %all-to-all-done.2) | copy-start | bytes 786436
  29.1 57.7 %all-to-all-start = ((bf16[128,4,2048]{2,0,1:T(8,128)(2,1)}), bf16[128,4,2048]{2,0,1:T(8,128)(2,1)S(1)}, u32[]{:S(2)}, u32[]{:S(2)}) async-start(bf16[128,4,2048]{2,0,1:T(8,128)(2,1)} %copy.32), calls=%async_computation | async-start | bytes 4194304 | tf_op jit(solution)/shard_map/all_to_all | solution.py:99
  33.3 256.6 %all-gather.3.cloned.1.call-start = ((), (), s32[]{:S(2)}) async-start(), calls=%async_computation.5 | async-start | bytes 20971520 | tf_op jit(solution)/shard_map/all_gather | solution.py:110
  38.0 43.0 %collective-permute-start = (bf16[128,2048]{0,1:T(8,128)(2,1)}, bf16[128,2048]{0,1:T(8,128)(2,1)}, u32[]{:S(2)}, u32[]{:S(2)}) collective-permute-start(bf16[128,2048]{0,1:T(8,128)(2,1)} %bitcast.136), channel_id=1, source_target_pairs={{0,1},{1,0},{2,3},{3,2},{4,5},{5,4},{6,7},{7,6},{8,9},{9,8},{10,11... | collective-permute-start | bytes 1572872 | tf_op jit(solution)/shard_map/ppermute | solution.py:21
  42.1 40.9 %collective-permute-start.1 = (bf16[128,2048]{0,1:T(8,128)(2,1)}, bf16[128,2048]{0,1:T(8,128)(2,1)}, u32[]{:S(2)}, u32[]{:S(2)}) collective-permute-start(bf16[128,2048]{0,1:T(8,128)(2,1)} %bitcast.135), channel_id=1, source_target_pairs={{0,2},{1,3},{2,0},{3,1},{4,6},{5,7},{6,4},{7,5},{8,10},{9,11},{10,... | collective-permute-start | bytes 1572872 | tf_op jit(solution)/shard_map/ppermute | solution.py:21
  44.5 40.4 %collective-permute-start.2 = (bf16[128,2048]{0,1:T(8,128)(2,1)}, bf16[128,2048]{0,1:T(8,128)(2,1)}, u32[]{:S(2)}, u32[]{:S(2)}) collective-permute-start(bf16[128,2048]{0,1:T(8,128)(2,1)} %bitcast.134), channel_id=1, source_target_pairs={{0,3},{1,2},{2,1},{3,0},{4,7},{5,6},{6,5},{7,4},{8,11},{9,10},{10,... | collective-permute-start | bytes 1572872 | tf_op jit(solution)/shard_map/ppermute | solution.py:21
  44.5 2.6 copy-start.10
  44.8 36.1 %copy-start.4 = (bf16[128,4,256]{2,0,1:T(8,128)(2,1)S(1)}, bf16[128,4,256]{2,0,1:T(8,128)(2,1)}, u32[]{:S(2)}) copy-start(bf16[128,4,256]{2,0,1:T(8,128)(2,1)} %copy-done.3) | copy-start | bytes 786436
  86.9 13.4 %copy-start.2 = (bf16[1,128,8192]{2,1,0:T(8,128)(2,1)S(1)}, bf16[1,128,8192]{2,1,0:T(8,128)(2,1)}, u32[]{:S(2)}) copy-start(bf16[1,128,8192]{2,1,0:T(8,128)(2,1)} %param.14) | copy-start | bytes 6291460
  104.4 4.8 %copy-start = (bf16[2,512,128]{2,1,0:T(8,128)(2,1)}, bf16[2,512,128]{2,1,0:T(8,128)(2,1)S(1)}, u32[]{:S(2)}) copy-start(bf16[2,512,128]{2,1,0:T(8,128)(2,1)S(1)} %get-tuple-element.441) | copy-start | bytes 786436 | tf_op jit(solution)/shard_map/while
  157.4 2.4 copy-start.5
  157.4 2.4 copy-start.8
  157.4 3.2 %copy-start.1 = (bf16[2,512,128]{2,1,0:T(8,128)(2,1)S(1)}, bf16[2,512,128]{2,1,0:T(8,128)(2,1)}, u32[]{:S(2)}) copy-start(bf16[2,512,128]{2,1,0:T(8,128)(2,1)} %copy-done) | copy-start | bytes 786436 | tf_op jit(solution)/shard_map/while
  160.6 4.8 %copy-start = (bf16[2,512,128]{2,1,0:T(8,128)(2,1)}, bf16[2,512,128]{2,1,0:T(8,128)(2,1)S(1)}, u32[]{:S(2)}) copy-start(bf16[2,512,128]{2,1,0:T(8,128)(2,1)S(1)} %get-tuple-element.441) | copy-start | bytes 786436 | tf_op jit(solution)/shard_map/while
  213.5 2.4 copy-start.5
  213.5 2.4 copy-start.8
  213.5 3.2 %copy-start.1 = (bf16[2,512,128]{2,1,0:T(8,128)(2,1)S(1)}, bf16[2,512,128]{2,1,0:T(8,128)(2,1)}, u32[]{:S(2)}) copy-start(bf16[2,512,128]{2,1,0:T(8,128)(2,1)} %copy-done) | copy-start | bytes 786436 | tf_op jit(solution)/shard_map/while
  218.8 12.8 %all-to-all-start.4 = ((bf16[4,128,256]{2,1,0:T(8,128)(2,1)}), bf16[4,128,256]{2,1,0:T(8,128)(2,1)S(1)}, u32[]{:S(2)}, u32[]{:S(2)}) async-start(bf16[4,128,256]{2,1,0:T(8,128)(2,1)} %all_to_all.72), calls=%async_computation.4 | async-start | bytes 524288 | tf_op jit(solution)/shard_map/all_to_all | solution.py:107
  227.7 7.6 %copy-start.7 = (bf16[2,512,128]{2,1,0:T(8,128)(2,1)S(1)}, bf16[2,512,128]{2,1,0:T(8,128)(2,1)}, u32[]{:S(2)}) copy-start(bf16[2,512,128]{2,1,0:T(8,128)(2,1)} %get-tuple-element.103) | copy-start | bytes 786436
  231.6 51.8 %all-to-all-start.3 = ((bf16[4,128,2048]{2,1,0:T(8,128)(2,1)}), bf16[4,128,2048]{2,1,0:T(8,128)(2,1)S(1)}, u32[]{:S(2)}, u32[]{:S(2)}) async-start(bf16[4,128,2048]{2,1,0:T(8,128)(2,1)} %all_to_all.69), calls=%async_computation.3 | async-start | bytes 4194304 | tf_op jit(solution)/shard_map/all_to_all | solution.py:106
  236.2 8.6 %collective-permute-start.4 = (bf16[512,256]{0,1:T(8,128)(2,1)}, bf16[512,256]{0,1:T(8,128)(2,1)S(1)}, u32[]{:S(2)}, u32[]{:S(2)}) collective-permute-start(bf16[512,256]{0,1:T(8,128)(2,1)} %bitcast.22), channel_id=1, source_target_pairs={{0,28},{4,24},{8,20},{12,16},{16,12},{20,8},{24,4},{28,0},{1,29},{... | collective-permute-start | bytes 786440 | tf_op jit(solution)/shard_map/ppermute | solution.py:111
  (4 other events, 3.0 us)
Sparse Core Ops, SparseCore 0:
  104.5 182.8 all-gather.2
